TPU v7x, 256 devices: a whole 4x4x8 slice. The times are simulated.
256 devices in a mesh: section: 2 (over x_hi), ctx: 32 (over z, x_lo, core), mp: 4 (over y).
Axes of the slice: x: 4 (x_hi: 2, x_lo: 2; x = x_hi * 2 + x_lo), y: 4, z: 8, core: 2. Of those that a mesh axis runs over, the one named last changes fastest.
Arguments:
- queries: bfloat16 [2, 8192, 4096], P('section', 'ctx', 'mp'), may hold values from -130 to 130
- keys: bfloat16 [2, 8192, 512], P('section', 'ctx', 'mp'), may hold values from -4.5 to 4.5
- values: bfloat16 [2, 8192, 512], P('section', 'ctx', 'mp'), may hold values from -6 to 6
- doc_lengths: int32 [2, 16], P('section'), may hold values from 1 to 4096, 8192 in all within a row
Outputs:
- attended: bfloat16 [2, 8192, 4096], P('section', ('ctx', 'mp'))
- passed: bfloat16 [2, 8192, 4096], P('section', ('ctx', 'mp'))
All inputs are finite; a program needn't handle non-finite values.
Results may differ from a plain program's by a relative error of at most 0.004.
Values may be sent and summed in bfloat16 or wider, within the bound.
No kernel may reach another device: no remote copies, remote signals or barrier semaphores. Data moves between devices by JAX's collectives and lax.ppermute only.
A program may use at most 192 MiB of HBM per device.

v0:
```python
import functools
import math

import jax
import jax.numpy as jnp
from jax import lax
from jax.experimental import pallas as pl
from jax.experimental.pallas import tpu as pltpu
from jax.sharding import PartitionSpec as P

DH = 128
LOG2E = 1.4426950408889634
DOCS = 16
MOST = 4096
BK = 512


def doc_of(positions, ends):
    return jnp.sum((positions[:, None] >= ends[None, :]).astype(jnp.int32), axis=1)


def flash_kernel(bounds_ref, qt_ref, kv_ref, qdoc_ref, qpos_ref, fac_ref, kdoc_ref,
                 o_ref, m_sc, l_sc, acc_sc, *, heads, rows, bk, steps, copies):
    j = pl.program_id(0)
    lo = bounds_ref[0]
    hi = bounds_ref[1]

    @pl.when(j == 0)
    def _():
        m_sc[...] = jnp.full(m_sc.shape, -1e30, jnp.float32)
        l_sc[...] = jnp.zeros(l_sc.shape, jnp.float32)
        acc_sc[...] = jnp.zeros(acc_sc.shape, jnp.float32)

    blk = lo + j
    full = bounds_ref[2 + j] == 1

    def step(masked):
        k = kv_ref[:, :DH]
        vt = kv_ref[:, DH:].T
        fac = jnp.concatenate([fac_ref[...]] * heads, axis=1)
        s = jnp.dot(k, qt_ref[...], preferred_element_type=jnp.float32)
        s = s * (fac * LOG2E)
        if masked:
            kpos = blk * bk + lax.broadcasted_iota(jnp.int32, (bk, 1), 0)
            allowed = (kdoc_ref[...] == qdoc_ref[...]) & (kpos <= qpos_ref[...])
            allowed = jnp.concatenate([allowed] * heads, axis=1)
            s = jnp.where(allowed, s, -1e30)
        m_old = m_sc[...]
        m_new = jnp.maximum(m_old, jnp.max(s, axis=0, keepdims=True))
        alpha = jnp.exp2(m_old - m_new)
        p = jnp.exp2(s - m_new)
        if masked:
            p = jnp.where(allowed, p, 0.0)
        l_sc[...] = alpha * l_sc[...] + jnp.sum(p, axis=0, keepdims=True)
        pv = jnp.dot(vt, p.astype(jnp.bfloat16), preferred_element_type=jnp.float32)
        acc_sc[...] = alpha * acc_sc[...] + pv
        m_sc[...] = m_new

    @pl.when((blk <= hi) & full)
    def _():
        step(False)

    @pl.when((blk <= hi) & jnp.logical_not(full))
    def _():
        step(True)

    @pl.when(j == steps - 1)
    def _():
        for h in range(heads):
            cols = slice(h * rows, (h + 1) * rows)
            out = (acc_sc[:, cols] / l_sc[:, cols]).T.astype(o_ref.dtype)
            for c in range(copies):
                o_ref[c, :, h * DH:(h + 1) * DH] = out


def attend(bounds, query_rows, kv, query_doc, query_pos, factor, key_doc, steps, bk, copies):
    rows, width = query_rows.shape
    heads = width // DH
    qt = query_rows.reshape(rows, heads, DH).transpose(2, 1, 0).reshape(DH, heads * rows)

    def kv_map(j, b):
        return (jnp.minimum(b[0] + j, b[1]), 0)

    whole = lambda j, b: (0, 0)
    return pl.pallas_call(
        functools.partial(flash_kernel, heads=heads, rows=rows, bk=bk, steps=steps,
                          copies=copies),
        out_shape=jax.ShapeDtypeStruct((copies, rows, width), jnp.bfloat16),
        grid_spec=pltpu.PrefetchScalarGridSpec(
            num_scalar_prefetch=1,
            grid=(steps,),
            in_specs=[
                pl.BlockSpec((DH, heads * rows), whole),
                pl.BlockSpec((bk, 2 * DH), kv_map),
                pl.BlockSpec((1, rows), whole),
                pl.BlockSpec((1, rows), whole),
                pl.BlockSpec((1, rows), whole),
                pl.BlockSpec((bk, 1), kv_map),
            ],
            out_specs=pl.BlockSpec((copies, rows, width), lambda j, b: (0, 0, 0)),
            scratch_shapes=[
                pltpu.VMEM((1, heads * rows), jnp.float32),
                pltpu.VMEM((1, heads * rows), jnp.float32),
                pltpu.VMEM((DH, heads * rows), jnp.float32),
            ],
        ),
        compiler_params=pltpu.CompilerParams(dimension_semantics=("arbitrary",)),
    )(bounds, qt, kv, query_doc.reshape(1, rows), query_pos.reshape(1, rows),
      factor.reshape(1, rows), key_doc.reshape(-1, 1))


def body(queries, keys, values, doc_lengths):
    query_rows = queries[0]
    key_rows = keys[0]
    value_rows = values[0]
    lengths = doc_lengths[0]
    rows = query_rows.shape[0]
    cycle = lax.axis_size("ctx")
    count = rows * cycle
    base_len = count // 16
    position = lax.axis_index("ctx")
    first = position * rows
    ends = jnp.cumsum(lengths)
    starts = ends - lengths
    query_pos = first + jnp.arange(rows, dtype=jnp.int32)
    query_doc = doc_of(query_pos, ends)
    lookup = query_doc[:, None] == jnp.arange(DOCS, dtype=jnp.int32)[None, :]
    query_len = jnp.sum(jnp.where(lookup, lengths[None, :], 0), axis=1).astype(jnp.float32)
    factor = jnp.maximum(1.0, jnp.log(query_len) / math.log(float(base_len))) * (
        1.0 / math.sqrt(DH)
    )
    bk = min(BK, count)
    span = max(
        (c * rows + rows - 1) // bk - max(0, c * rows - (MOST - 1)) // bk + 1
        for c in range(cycle)
    )
    first_doc = jnp.sum((first >= ends).astype(jnp.int32))
    lo = jnp.sum(jnp.where(jnp.arange(DOCS) == first_doc, starts, 0)) // bk
    hi = (first + rows - 1) // bk
    last_doc = jnp.sum((first + rows - 1 >= ends).astype(jnp.int32))
    block_first = jnp.minimum(lo + jnp.arange(span, dtype=jnp.int32), hi) * bk
    block_last = block_first + bk - 1
    full = (
        (doc_of(block_first, ends) == first_doc)
        & (doc_of(block_last, ends) == first_doc)
        & (last_doc == first_doc)
        & (block_last <= first)
    )
    bounds = jnp.concatenate([jnp.stack([lo, hi]), full.astype(jnp.int32)]).astype(jnp.int32)
    kv_rows = jnp.concatenate([key_rows, value_rows], axis=1)
    kv = lax.all_gather(kv_rows, "ctx", axis=0, tiled=True)
    key_doc = doc_of(jnp.arange(count, dtype=jnp.int32), ends)[None, :]
    sections = lax.axis_size("section")
    result = attend(
        bounds, query_rows, kv, query_doc[:, None], query_pos[:, None], factor[:, None],
        key_doc, span, bk, sections,
    )
    share = lax.axis_size("mp")
    width = result.shape[2]
    got = lax.all_to_all(
        result.reshape(sections * rows, width), ("section", "mp"), 0, 1, tiled=True
    )
    here = lax.axis_index("section")
    behind = (here + sections - 1) % sections
    span_cols = share * width
    own = lax.dynamic_slice_in_dim(got, here * span_cols, span_cols, axis=1)
    moved = lax.dynamic_slice_in_dim(got, behind * span_cols, span_cols, axis=1)
    return (own[None], moved[None])


def solution(mesh):
    return jax.shard_map(
        body,
        mesh=mesh,
        in_specs=(
            P("section", "ctx", "mp"),
            P("section", "ctx", "mp"),
            P("section", "ctx", "mp"),
            P("section", None),
        ),
        out_specs=(P("section", ("ctx", "mp"), None), P("section", ("ctx", "mp"), None)),
        check_vma=False,
    )
```

profile of v0, /device:TPU:128, one launch (start us, length us, event | category | flops | bytes accessed | tf_op | source)
XLA Modules:
  0.0 124.4 jit_solution(5207456244046172352)
XLA Ops:
  7.2 0.0 copy-start.2
  7.2 0.0 copy-start
  7.2 0.0 all-gather.2.cloned.1.call-start
  7.2 1.6 %pad_maximum_fusion = bf16[256,256]{1,0:T(8,128)(2,1)} fusion(bf16[256,128]{1,0:T(8,128)(2,1)} %bitcast.32, bf16[256,128]{1,0:T(8,128)(2,1)} %bitcast.33), kind=kLoop, calls=%fused_computation.4 | loop fusion | flops 262144 | bytes 262144 | tf_op jit(solution)/shard_map/concatenate | solution.py:150
  8.8 0.0 all-gather.2.cloned.1.call-update
  8.9 0.7 copy.16
  9.6 0.1 reduce
  9.7 0.6 fusion
  10.4 1.9 %fusion.2 = (s32[]{:T(128)}, s32[]{:T(128)}) fusion(s32[16]{0:T(128)S(1)} %reduce, s32[]{:T(128)S(6)} %sub.24, s32[1,16]{1,0:T(1,128)} %param.7, s32[]{:T(128)} %fusion), kind=kLoop, calls=%fused_computation.19 | loop fusion | flops 110 | bytes 144 | tf_op jit(solution)/shard_map/reduce_sum | solution.py:140
  15.9 0.2 convert_reduce_fusion
  16.1 2.7 %copy.18.kdoc_ref = s32[8192,1]{1,0:T(8,128)} copy(s32[8192,1]{0,1:T(1,128)S(1)} %bitcast.31) | data formatting | bytes 65536 | tf_op jit(solution)/shard_map/reshape;broadcast_in_dim | solution.py:109
  18.8 0.0 copy-done
  18.8 0.1 copy.21
  18.9 0.6 copy.17
  19.5 0.9 copy.22
  20.4 0.2 convert_reduce_fusion.3
  20.6 0.6 and_convert_fusion
  21.1 0.7 pad_add_fusion.bounds_ref
  21.8 0.6 iota_add_fusion.qpos_ref
  22.4 0.1 convert_reduce_fusion.1
  22.5 0.0 copy-start.1
  22.5 0.0 copy-done.2
  22.5 0.1 select_reduce_fusion
  22.6 0.6 maximum_multiply_fusion
  23.2 54.0 %all-gather.2.cloned.1.call-done.kv_ref = bf16[8192,256]{1,0:T(8,128)(2,1)} async-done(((bf16[256,256]{1,0:T(8,128)(2,1)}), bf16[8192,256]{1,0:T(8,128)(2,1)}) %all-gather.2.cloned.1.call-update) | async-done | bytes 4194320 | tf_op jit(solution)/shard_map/all_gather | solution.py:151
  77.1 0.0 copy-done.1
  77.1 15.0 %shard_map.59 = bf16[2,256,1024]{2,1,0:T(8,128)(2,1)} custom-call(s32[11]{0:T(128)} %pad_add_fusion.bounds_ref, bf16[128,2048]{1,0:T(8,128)(2,1)} %bitcast.27, bf16[8192,256]{1,0:T(8,128)(2,1)} %all-gather.2.cloned.1.call-done.kv_ref, s32[1,256]{1,0:T(1,128)} %bitcast.34, s32[1,256]{1,0:T(1,128)} %iota_add_fusion.qpos_ref, f32[1,256]{1,0:T(1,128)} %bitcast.37, ...), custom_call_target="tpu_custom_call" | custom-call | tf_op jit(solution)/shard_map/pallas_call | solution.py:85
  92.1 8.4 %all-to-all-start = ((bf16[8,64,1024]{2,1,0:T(8,128)(2,1)}), bf16[8,64,1024]{2,1,0:T(8,128)(2,1)S(1)}, u32[]{:S(2)}, u32[]{:S(2)}) async-start(bf16[8,64,1024]{2,1,0:T(8,128)(2,1)} %bitcast.24), calls=%async_computation | async-start | bytes 2097152 | tf_op jit(solution)/shard_map/all_to_all | solution.py:160
  100.6 15.9 %all-to-all-done = bf16[8,64,1024]{2,1,0:T(8,128)(2,1)S(1)} async-done(((bf16[8,64,1024]{2,1,0:T(8,128)(2,1)}), bf16[8,64,1024]{2,1,0:T(8,128)(2,1)S(1)}, u32[]{:S(2)}, u32[]{:S(2)}) %all-to-all-start) | async-done | bytes 1048608 | tf_op jit(solution)/shard_map/all_to_all | solution.py:160
  116.4 0.1 copy.20
  116.5 1.0 dynamic-slice_bitcast_fusion
  (3 shorter events, 0.0 us)
Async XLA Ops:
  7.2 15.3 %copy-start.2 = (s32[1,16]{1,0:T(1,128)S(1)}, s32[1,16]{1,0:T(1,128)}, u32[]{:S(2)}) copy-start(s32[1,16]{1,0:T(1,128)} %param.7) | copy-start | bytes 196
  7.2 11.6 %copy-start = (bf16[1,256,1024]{2,1,0:T(8,128)(2,1)S(1)}, bf16[1,256,1024]{2,1,0:T(8,128)(2,1)}, u32[]{:S(2)}) copy-start(bf16[1,256,1024]{2,1,0:T(8,128)(2,1)} %param.4) | copy-start | bytes 1572868
  7.2 70.0 %all-gather.2.cloned.1.call-start = ((), (), s32[]{:S(2)}) async-start(), calls=%async_computation.1 | async-start | bytes 4325376 | tf_op jit(solution)/shard_map/all_gather | solution.py:151
  22.5 54.7 %copy-start.1 = (s32[256]{0:T(256)}, s32[256]{0:T(256)S(1)}, u32[]{:S(2)}) copy-start(s32[256]{0:T(256)S(1)} %convert_reduce_fusion.1) | copy-start | bytes 3076
  92.1 24.3 %all-to-all-start = ((bf16[8,64,1024]{2,1,0:T(8,128)(2,1)}), bf16[8,64,1024]{2,1,0:T(8,128)(2,1)S(1)}, u32[]{:S(2)}, u32[]{:S(2)}) async-start(bf16[8,64,1024]{2,1,0:T(8,128)(2,1)} %bitcast.24), calls=%async_computation | async-start | bytes 2097152 | tf_op jit(solution)/shard_map/all_to_all | solution.py:160
Sparse Core Ops, SparseCore 0:
  10.4 66.6 all-gather.1
where the time goes:
time: 127 us; the launch traced here: 124 us
  waiting for transfers between devices  69.8 us (55%)
  between operations  17.8 us (14%)
  Pallas kernels  15 us (12%)
  starting transfers between devices  8.49 us (7%)
  other arithmetic  7.2 us (6%)
  local copies, waits for them, and re-layouts  6.11 us (5%)
    all_gather x1, waiting for transfers between devices, body(): kv = lax.all_gather(kv_rows, 'ctx', axis=0, tiled=True)  54 us
    all_to_all x1, waiting for transfers between devices, body(): lax.all_to_all(result.reshape(sections * rows, width), ('section', 'mp'),...  15.9 us
    pallas_call x1, Pallas kernels, attend(): pl.pallas_call(functools.partial(flash_kernel, heads=heads, rows=rows, bk...  15 us
    all_to_all x1, starting transfers between devices, body(): lax.all_to_all(result.reshape(sections * rows, width), ('section', 'mp'),...  8.45 us
    another operation x1, local copies, waits for them, and re-layouts, attend(): key_doc.reshape(-1, 1)  2.67 us
  transfers between devices with their start and end apart: 2, of which 2 were waited for; matrix products, arithmetic and copies ran while one was open for 9% of the time, Pallas kernels for 0%

commit v1 on v0

v1 whole, which is shorter than its diff:
```python
import functools
import math

import jax
import jax.numpy as jnp
from jax import lax
from jax.experimental import pallas as pl
from jax.experimental.pallas import tpu as pltpu
from jax.sharding import PartitionSpec as P

DH = 128
LOG2E = 1.4426950408889634
DOCS = 16
MOST = 4096
BK = 512


def doc_of(positions, ends):
    return jnp.sum((positions[:, None] >= ends[None, :]).astype(jnp.int32), axis=1)


def update(k, vt, qt, fac, allowed, m_ref, l_ref, acc_ref):
    s = jnp.dot(k, qt, preferred_element_type=jnp.float32)
    s = s * (fac * LOG2E)
    if allowed is not None:
        s = jnp.where(allowed, s, -1e30)
    m_old = m_ref[...]
    m_new = jnp.maximum(m_old, jnp.max(s, axis=0, keepdims=True))
    alpha = jnp.exp2(m_old - m_new)
    p = jnp.exp2(s - m_new)
    if allowed is not None:
        p = jnp.where(allowed, p, 0.0)
    l_ref[...] = alpha * l_ref[...] + jnp.sum(p, axis=0, keepdims=True)
    pv = jnp.dot(vt, p.astype(jnp.bfloat16), preferred_element_type=jnp.float32)
    acc_ref[...] = alpha * acc_ref[...] + pv
    m_ref[...] = m_new


def local_kernel(qt_ref, kv_ref, qdoc_ref, qpos_ref, fac_ref, kdoc_ref, kpos_ref,
                 m_ref, l_ref, acc_ref, *, heads):
    m_ref[...] = jnp.full(m_ref.shape, -1e30, jnp.float32)
    l_ref[...] = jnp.zeros(l_ref.shape, jnp.float32)
    acc_ref[...] = jnp.zeros(acc_ref.shape, jnp.float32)
    allowed = (kdoc_ref[...] == qdoc_ref[...]) & (kpos_ref[...] <= qpos_ref[...])
    allowed = jnp.concatenate([allowed] * heads, axis=1)
    fac = jnp.concatenate([fac_ref[...]] * heads, axis=1)
    update(kv_ref[:, :DH], kv_ref[:, DH:].T, qt_ref[...], fac, allowed, m_ref, l_ref, acc_ref)


def far_kernel(plan_ref, qt_ref, kv_ref, qdoc_ref, fac_ref, kdoc_ref, m0_ref, l0_ref, acc0_ref,
               o_ref, m_sc, l_sc, acc_sc, *, heads, rows, bk, steps, copies):
    j = pl.program_id(0)
    start = plan_ref[j]
    limit = plan_ref[steps + j]
    mode = plan_ref[2 * steps + j]

    @pl.when(j == 0)
    def _():
        m_sc[...] = m0_ref[...]
        l_sc[...] = l0_ref[...]
        acc_sc[...] = acc0_ref[...]

    def step(masked):
        fac = jnp.concatenate([fac_ref[...]] * heads, axis=1)
        allowed = None
        if masked:
            kpos = start + lax.broadcasted_iota(jnp.int32, (bk, 1), 0)
            allowed = (kdoc_ref[...] == qdoc_ref[...]) & (kpos < limit)
            allowed = jnp.concatenate([allowed] * heads, axis=1)
        update(kv_ref[:, :DH], kv_ref[:, DH:].T, qt_ref[...], fac, allowed, m_sc, l_sc, acc_sc)

    @pl.when(mode == 2)
    def _():
        step(False)

    @pl.when(mode == 1)
    def _():
        step(True)

    @pl.when(j == steps - 1)
    def _():
        for h in range(heads):
            cols = slice(h * rows, (h + 1) * rows)
            out = (acc_sc[:, cols] / l_sc[:, cols]).T.astype(o_ref.dtype)
            for c in range(copies):
                o_ref[c, :, h * DH:(h + 1) * DH] = out


def attend(plan, query_rows, kv_local, kv, query_doc, query_pos, factor, local_doc, key_doc,
           steps, bk, copies):
    rows, width = query_rows.shape
    heads = width // DH
    qt = query_rows.reshape(rows, heads, DH).transpose(2, 1, 0).reshape(DH, heads * rows)
    qdoc = query_doc.reshape(1, rows)
    fac = factor.reshape(1, rows)
    state = [
        jax.ShapeDtypeStruct((1, heads * rows), jnp.float32),
        jax.ShapeDtypeStruct((1, heads * rows), jnp.float32),
        jax.ShapeDtypeStruct((DH, heads * rows), jnp.float32),
    ]
    m0, l0, acc0 = pl.pallas_call(
        functools.partial(local_kernel, heads=heads),
        out_shape=state,
    )(qt, kv_local, qdoc, query_pos.reshape(1, rows), fac, local_doc.reshape(-1, 1),
      query_pos.reshape(-1, 1))

    def kv_map(j, p):
        return (pl.multiple_of(p[j], rows), 0)

    whole = lambda j, p: (0, 0)
    return pl.pallas_call(
        functools.partial(far_kernel, heads=heads, rows=rows, bk=bk, steps=steps,
                          copies=copies),
        out_shape=jax.ShapeDtypeStruct((copies, rows, width), jnp.bfloat16),
        grid_spec=pltpu.PrefetchScalarGridSpec(
            num_scalar_prefetch=1,
            grid=(steps,),
            in_specs=[
                pl.BlockSpec((DH, heads * rows), whole),
                pl.BlockSpec((pl.Element(bk), pl.Element(2 * DH)), kv_map),
                pl.BlockSpec((1, rows), whole),
                pl.BlockSpec((1, rows), whole),
                pl.BlockSpec((pl.Element(bk), pl.Element(1)), kv_map),
                pl.BlockSpec((1, heads * rows), whole),
                pl.BlockSpec((1, heads * rows), whole),
                pl.BlockSpec((DH, heads * rows), whole),
            ],
            out_specs=pl.BlockSpec((copies, rows, width), lambda j, p: (0, 0, 0)),
            scratch_shapes=[
                pltpu.VMEM((1, heads * rows), jnp.float32),
                pltpu.VMEM((1, heads * rows), jnp.float32),
                pltpu.VMEM((DH, heads * rows), jnp.float32),
            ],
        ),
        compiler_params=pltpu.CompilerParams(dimension_semantics=("arbitrary",)),
    )(plan, qt, kv, qdoc, fac, key_doc.reshape(-1, 1), m0, l0, acc0)


def body(queries, keys, values, doc_lengths):
    query_rows = queries[0]
    key_rows = keys[0]
    value_rows = values[0]
    lengths = doc_lengths[0]
    rows = query_rows.shape[0]
    cycle = lax.axis_size("ctx")
    count = rows * cycle
    base_len = count // 16
    position = lax.axis_index("ctx")
    first = position * rows
    ends = jnp.cumsum(lengths)
    starts = ends - lengths
    query_pos = first + jnp.arange(rows, dtype=jnp.int32)
    query_doc = doc_of(query_pos, ends)
    lookup = query_doc[:, None] == jnp.arange(DOCS, dtype=jnp.int32)[None, :]
    query_len = jnp.sum(jnp.where(lookup, lengths[None, :], 0), axis=1).astype(jnp.float32)
    factor = jnp.maximum(1.0, jnp.log(query_len) / math.log(float(base_len))) * (
        1.0 / math.sqrt(DH)
    )
    bk = min(BK, count)
    steps = max(1, max(-(-min(c * rows, MOST - 1) // bk) for c in range(cycle)))
    first_doc = jnp.sum((first >= ends).astype(jnp.int32))
    last_doc = jnp.sum((first + rows - 1 >= ends).astype(jnp.int32))
    doc_start = jnp.sum(jnp.where(jnp.arange(DOCS) == first_doc, starts, 0))
    need = (first - doc_start + bk - 1) // bk
    back = steps - jnp.arange(steps, dtype=jnp.int32)
    back = jnp.maximum(jnp.minimum(back, need), 1)
    limit = first - bk * (back - 1)
    raw = limit - bk
    start = jnp.maximum(raw, 0)
    active = (steps - jnp.arange(steps, dtype=jnp.int32)) <= need
    full = active & (raw >= doc_start) & (last_doc == first_doc)
    mode = jnp.where(full, 2, jnp.where(active, 1, 0))
    plan = jnp.concatenate([start, limit, mode]).astype(jnp.int32)
    kv_rows = jnp.concatenate([key_rows, value_rows], axis=1)
    kv = lax.all_gather(kv_rows, "ctx", axis=0, tiled=True)
    key_doc = doc_of(jnp.arange(count, dtype=jnp.int32), ends)
    sections = lax.axis_size("section")
    result = attend(
        plan, query_rows, kv_rows, kv, query_doc, query_pos, factor, query_doc, key_doc,
        steps, bk, sections,
    )
    share = lax.axis_size("mp")
    width = result.shape[2]
    got = lax.all_to_all(
        result.reshape(sections * rows, width), ("section", "mp"), 0, 1, tiled=True
    )
    here = lax.axis_index("section")
    behind = (here + sections - 1) % sections
    span_cols = share * width
    own = lax.dynamic_slice_in_dim(got, here * span_cols, span_cols, axis=1)
    moved = lax.dynamic_slice_in_dim(got, behind * span_cols, span_cols, axis=1)
    return (own[None], moved[None])


def solution(mesh):
    return jax.shard_map(
        body,
        mesh=mesh,
        in_specs=(
            P("section", "ctx", "mp"),
            P("section", "ctx", "mp"),
            P("section", "ctx", "mp"),
            P("section", None),
        ),
        out_specs=(P("section", ("ctx", "mp"), None), P("section", ("ctx", "mp"), None)),
        check_vma=False,
    )
```

time: 127 us -> 126 us (level); the launches traced: 124 us -> 125 us
  starting transfers between devices: 8.49 us -> 15.4 us
  waiting for transfers between devices: 69.8 us -> 64.4 us
  local copies, waits for them, and re-layouts: 6.11 us -> 7.94 us
  Pallas kernels: 15 us -> 13.2 us
  between operations: 17.8 us -> 16 us
    all_to_all x1, starting transfers between devices: 8.45 us -> 15.4 us  [body(): lax.all_to_all(result.reshape(sections * rows, width), ('section', 'mp'),...]
    all_gather x1, waiting for transfers between devices: 54 us -> 49.8 us  [body(): kv = lax.all_gather(kv_rows, 'ctx', axis=0, tiled=True)]
    another operation x2 -> x1, local copies, waits for them, and re-layouts: 3.4 us -> 0.73 us  [the longest x1 2.67 us: attend(): key_doc.reshape(-1, 1)]
    reshape x0 -> x1, local copies, waits for them, and re-layouts: none -> 2.67 us  [attend(): key_doc.reshape(-1, 1)]
    pallas_call x1 -> x2, Pallas kernels: 15 us -> 13.2 us  [the longest x1 9.69 us: attend(): pl.pallas_call(functools.partial(far_kernel, heads=heads, rows=rows, bk=b...]
  transfers between devices with their start and end apart: 2 -> 2, of which waited for: 2 -> 2; matrix products, arithmetic and copies ran while one was open for 9% -> 10% of each run, Pallas kernels for 0% -> 3%
where the time goes in v1:
time: 126 us; the launch traced here: 125 us
  waiting for transfers between devices  64.4 us (51%)
  between operations  16 us (13%)
  starting transfers between devices  15.4 us (12%)
  Pallas kernels  13.2 us (10%)
  local copies, waits for them, and re-layouts  7.94 us (6%)
  other arithmetic  7.77 us (6%)
    all_gather x1, waiting for transfers between devices, body(): kv = lax.all_gather(kv_rows, 'ctx', axis=0, tiled=True)  49.8 us
    all_to_all x1, starting transfers between devices, body(): lax.all_to_all(result.reshape(sections * rows, width), ('section', 'mp'),...  15.4 us
    all_to_all x1, waiting for transfers between devices, body(): lax.all_to_all(result.reshape(sections * rows, width), ('section', 'mp'),...  14.6 us
    pallas_call x1, Pallas kernels, attend(): pl.pallas_call(functools.partial(far_kernel, heads=heads, rows=rows, bk=b...  9.69 us
    pallas_call x1, Pallas kernels, attend(): pl.pallas_call(functools.partial(local_kernel, heads=heads), out_shape=st...  3.47 us
    reshape x1, local copies, waits for them, and re-layouts, attend(): key_doc.reshape(-1, 1)  2.67 us
  transfers between devices with their start and end apart: 2, of which 2 were waited for; matrix products, arithmetic and copies ran while one was open for 10% of the time, Pallas kernels for 3%

profile of v1, /device:TPU:128, one launch (start us, length us, event | category | flops | bytes accessed | tf_op | source)
XLA Modules:
  0.0 124.7 jit_solution(17728147026477668065)
XLA Ops:
  7.2 0.0 copy-start.1
  7.2 0.0 all-gather.2.cloned.1.call-start
  7.2 1.5 %pad_maximum_fusion.kv_ref = bf16[256,256]{1,0:T(8,128)(2,1)} fusion(bf16[256,128]{1,0:T(8,128)(2,1)} %bitcast.32, bf16[256,128]{1,0:T(8,128)(2,1)} %bitcast.33), kind=kLoop, calls=%fused_computation.4 | loop fusion | flops 262144 | bytes 262144 | tf_op jit(solution)/shard_map/concatenate | solution.py:174
  8.8 0.0 all-gather.2.cloned.1.call-update
  8.8 0.7 copy.18
  9.6 0.1 reduce
  9.7 0.6 fusion
  10.3 2.0 %fusion.1 = (s32[]{:T(128)}, s32[]{:T(128)}) fusion(s32[16]{0:T(128)S(1)} %reduce, s32[]{:T(128)} %fusion, s32[1,16]{1,0:T(1,128)} %param.7, s32[]{:T(128)S(6)} %sub.46), kind=kLoop, calls=%fused_computation.18 | loop fusion | flops 110 | bytes 144 | tf_op jit(solution)/shard_map/reduce_sum | solution.py:163
  14.2 0.1 convert_reduce_fusion.1
  14.3 0.0 copy-start
  14.3 0.8 copy.20.kdoc_ref
  15.1 1.1 copy.24
  16.3 0.6 copy.19
  16.8 0.9 copy.25
  17.7 0.2 convert_reduce_fusion
  17.9 2.7 %copy.21.kdoc_ref = s32[8192,1]{1,0:T(8,128)} copy(s32[8192,1]{0,1:T(1,128)S(1)} %bitcast.31) | data formatting | bytes 65536 | tf_op jit(solution)/shard_map/reshape | solution.py:136
  20.6 0.6 iota_add_fusion.1.qpos_ref
  21.2 0.0 copy-done.1
  21.2 0.1 select_reduce_fusion
  21.3 0.7 iota_add_fusion.kpos_ref
  21.9 0.6 maximum_multiply_fusion
  22.5 0.0 copy-done
  22.5 3.5 %shard_map.59 = (f32[1,2048]{1,0:T(1,128)}, f32[1,2048]{1,0:T(1,128)}, f32[128,2048]{1,0:T(8,128)}) custom-call(bf16[128,2048]{1,0:T(8,128)(2,1)} %bitcast.23, bf16[256,256]{1,0:T(8,128)(2,1)} %pad_maximum_fusion.kv_ref, s32[1,256]{1,0:T(1,128)} %bitcast.35, s32[1,256]{1,0:T(1,128)} %iota_add_fusion.1.qpos_ref, f32[1,256]{1,0:T(1,128)} %bitcast.37, ...), custom_call_target="tpu_custom_call" | custom-call | tf_op jit(solution)/shard_map/pallas_call | solution.py:101
  26.0 0.6 and_select_fusion
  26.6 0.6 pad_add_fusion.plan_ref
  27.2 49.8 %all-gather.2.cloned.1.call-done.kv_ref = bf16[8192,256]{1,0:T(8,128)(2,1)} async-done(((bf16[256,256]{1,0:T(8,128)(2,1)}), bf16[8192,256]{1,0:T(8,128)(2,1)}) %all-gather.2.cloned.1.call-update) | async-done | bytes 4194320 | tf_op jit(solution)/shard_map/all_gather | solution.py:175
  77.0 9.7 %shard_map.60 = bf16[2,256,1024]{2,1,0:T(8,128)(2,1)} custom-call(s32[24]{0:T(128)} %pad_add_fusion.plan_ref, bf16[128,2048]{1,0:T(8,128)(2,1)} %bitcast.24, bf16[8192,256]{1,0:T(8,128)(2,1)} %all-gather.2.cloned.1.call-done.kv_ref, s32[1,256]{1,0:T(1,128)} %bitcast.36, f32[1,256]{1,0:T(1,128)} %bitcast.38, s32[8192,1]{1,0:T(8,128)} %copy.21.kdoc_ref, ...), custom_call_target="tpu_custom_call" | custom-call | tf_op jit(solution)/shard_map/pallas_call | solution.py:111
  86.7 15.4 %all-to-all-start = ((bf16[8,64,1024]{2,1,0:T(8,128)(2,1)}), bf16[8,64,1024]{2,1,0:T(8,128)(2,1)S(1)}, u32[]{:S(2)}, u32[]{:S(2)}) async-start(bf16[8,64,1024]{2,1,0:T(8,128)(2,1)} %bitcast.25), calls=%async_computation | async-start | bytes 2097152 | tf_op jit(solution)/shard_map/all_to_all | solution.py:184
  102.1 14.6 %all-to-all-done = bf16[8,64,1024]{2,1,0:T(8,128)(2,1)S(1)} async-done(((bf16[8,64,1024]{2,1,0:T(8,128)(2,1)}), bf16[8,64,1024]{2,1,0:T(8,128)(2,1)S(1)}, u32[]{:S(2)}, u32[]{:S(2)}) %all-to-all-start) | async-done | bytes 1048608 | tf_op jit(solution)/shard_map/all_to_all | solution.py:184
  116.7 0.1 copy.23
  116.8 1.0 dynamic-slice_bitcast_fusion
  (3 shorter events, 0.0 us)
Async XLA Ops:
  7.2 14.0 %copy-start.1 = (s32[1,16]{1,0:T(1,128)S(1)}, s32[1,16]{1,0:T(1,128)}, u32[]{:S(2)}) copy-start(s32[1,16]{1,0:T(1,128)} %param.7) | copy-start | bytes 196
  7.2 69.8 %all-gather.2.cloned.1.call-start = ((), (), s32[]{:S(2)}) async-start(), calls=%async_computation.1 | async-start | bytes 4325376 | tf_op jit(solution)/shard_map/all_gather | solution.py:175
  14.3 8.2 %copy-start = (s32[256]{0:T(256)}, s32[256]{0:T(256)S(1)}, u32[]{:S(2)}) copy-start(s32[256]{0:T(256)S(1)} %convert_reduce_fusion.1) | copy-start | bytes 3076
  86.7 30.0 %all-to-all-start = ((bf16[8,64,1024]{2,1,0:T(8,128)(2,1)}), bf16[8,64,1024]{2,1,0:T(8,128)(2,1)S(1)}, u32[]{:S(2)}, u32[]{:S(2)}) async-start(bf16[8,64,1024]{2,1,0:T(8,128)(2,1)} %bitcast.25), calls=%async_computation | async-start | bytes 2097152 | tf_op jit(solution)/shard_map/all_to_all | solution.py:184
Sparse Core Ops, SparseCore 0:
  10.4 66.5 all-gather.1
